TPU v7x, 32 devices: a whole 2x2x4 slice. The times are simulated.
32 devices in a mesh: dp: 16 (over z, x, core), tm: 2 (over y).
Axes of the slice: x: 2, y: 2, z: 4, core: 2. Of those that a mesh axis runs over, the one named last changes fastest.
Arguments:
- src_mel: bfloat16 [2, 128, 640], P('tm', 'dp'), may hold values from -6 to 6
- owner: int32 [2, 128], P('tm', 'dp'), may hold values from 0 to 15, as said below
- dst_pos: int32 [2, 128], P('tm', 'dp'), may hold values from 0 to 7, as said below
- keep: int32 [2, 128], P('tm', 'dp'), may hold values 0 or 1
- cotangent: bfloat16 [16, 1024, 256], P('dp', 'tm'), may hold values from -0.125 to 0.125
- w_pre: bfloat16 [560, 512], replicated, may hold values from -0.25 to 0.25
- b_pre: float32 [512], replicated, may hold values from -3 to 3
- w_ups: bfloat16 [512, 4096], P('tm'), may hold values from -0.1875 to 0.1875
- upsample_bias: float32 [256], replicated, may hold values from -3 to 3
- w_res: bfloat16 [768, 256], replicated, may hold values from -0.21875 to 0.21875
- b_res: float32 [256], replicated, may hold values from -3 to 3
Outputs:
- section_out: bfloat16 [16, 1024, 256], P('dp', 'tm')
- grad_w_pre: float32 [560, 512], replicated
- grad_b_pre: float32 [512], replicated
- grad_w_res: float32 [768, 256], replicated
- grad_b_res: float32 [256], replicated
Inputs may be any that keep to these rules, and one draw needn't show every extreme that they name: Within one tm column, every dp index sends at most one of its segments to each owner, and every owner receives exactly 8 segments. `dst_pos`: the segments received by one owner in one column have positions 0 to 7, each once.
All inputs are finite; a program needn't handle non-finite values. No bound on the sum of `keep` on one device may be relied on, other than what follows from the above.
Results may differ from a plain program's by a relative error of at most 0.009.
The roundings to bfloat16 on the way count: a program that leaves them out, or rounds other values in their place, can miss the bound.
Values may be sent and summed in bfloat16 or wider, within the bound.
No kernel may reach another device: no remote copies, remote signals or barrier semaphores. Data moves between devices by JAX's collectives and lax.ppermute only.
A program may use at most 64 MiB of HBM per device.

v0:
```python
import jax
import jax.numpy as jnp
from jax import lax
from jax.sharding import PartitionSpec as P

KPRE = 7
UPSAMPLE_FACTOR = 8
DILATION_SIZE = 3


def with_halo(block, sides, width):
    for axis, dim in sides:
        count = lax.axis_size(axis)
        forward = [(i, i + 1) for i in range(count - 1)]
        backward = [(target, source) for source, target in forward]
        low = lax.ppermute(
            lax.slice_in_dim(block, block.shape[dim] - width, None, axis=dim), axis, forward
        )
        high = lax.ppermute(lax.slice_in_dim(block, 0, width, axis=dim), axis, backward)
        block = jnp.concatenate([low, block, high], axis=dim)
    return block


def leaky(value):
    return jnp.where(value > 0, value, 0.1 * value)


def negative_slope(value):
    return jnp.where(value > 0, 1.0, 0.1).astype(jnp.float32)


def contract_rows(left, right):
    return lax.dot_general(
        left, right, (((0,), (0,)), ((), ())), preferred_element_type=jnp.float32
    )


def contract_cols(left, right):
    return lax.dot_general(
        left, right, (((1,), (1,)), ((), ())), preferred_element_type=jnp.float32
    )


def local_pass(
    mel_ext,
    gradient_value,
    first_frame0,
    total,
    w_pre,
    b_pre,
    ups_forward,
    ups_backward,
    upsample_bias,
    w_res,
    b_res,
):
    mel_bins = mel_ext.shape[1]
    kpre = w_pre.shape[0] // mel_bins
    edge = kpre // 2 + 1
    frame_count = mel_ext.shape[0] - 2 * edge
    window_width = upsample_bias.shape[0]
    residual_kernel = w_res.shape[0] // window_width
    patches = jnp.concatenate([mel_ext[i : i + frame_count + 2] for i in range(kpre)], axis=1)
    pre = jnp.dot(patches, w_pre, preferred_element_type=jnp.float32) + b_pre
    frame_idx = first_frame0 - 1 + jnp.arange(frame_count + 2, dtype=jnp.int32)
    inside_f = ((frame_idx >= 0) & (frame_idx < total))[:, None]
    act = jnp.where(inside_f, leaky(pre), 0.0).astype(jnp.bfloat16)
    taps = ups_forward(act).reshape(frame_count + 2, 2 * UPSAMPLE_FACTOR, window_width)
    upper_output = taps[1:, :UPSAMPLE_FACTOR] + taps[:-1, UPSAMPLE_FACTOR:]
    sample_count = UPSAMPLE_FACTOR * frame_count
    start_offset = UPSAMPLE_FACTOR // 2 - DILATION_SIZE
    waveform = (
        upper_output.reshape(UPSAMPLE_FACTOR * (frame_count + 1), window_width)[
            start_offset : start_offset + sample_count + 2 * DILATION_SIZE
        ]
        + upsample_bias
    )
    step_index = (
        UPSAMPLE_FACTOR * first_frame0
        - DILATION_SIZE
        + jnp.arange(sample_count + 2 * DILATION_SIZE, dtype=jnp.int32)
    )
    inside_samples = ((step_index >= 0) & (step_index < UPSAMPLE_FACTOR * total))[:, None]
    hidden_state = jnp.where(inside_samples, leaky(waveform), 0.0).astype(jnp.bfloat16)
    column_block = jnp.concatenate(
        [
            hidden_state[kernel_index * DILATION_SIZE : kernel_index * DILATION_SIZE + sample_count]
            for kernel_index in range(residual_kernel)
        ],
        axis=1,
    )
    convolve_fn = jnp.dot(column_block, w_res, preferred_element_type=jnp.float32) + b_res
    output_rows = (waveform[DILATION_SIZE : DILATION_SIZE + sample_count] + convolve_fn).astype(
        jnp.bfloat16
    )
    g_wres = contract_rows(column_block, gradient_value)
    g_bres = jnp.sum(gradient_value.astype(jnp.float32), axis=0)
    backward_pass = contract_cols(gradient_value, w_res)
    hidden_gradient = jnp.zeros((sample_count + 2 * DILATION_SIZE, window_width), jnp.float32)
    for kernel_index in range(residual_kernel):
        hidden_gradient = hidden_gradient + jnp.pad(
            backward_pass[:, kernel_index * window_width : (kernel_index + 1) * window_width],
            (
                (
                    kernel_index * DILATION_SIZE,
                    (residual_kernel - 1 - kernel_index) * DILATION_SIZE,
                ),
                (0, 0),
            ),
        )
    waveform_gradient = jnp.where(
        inside_samples, hidden_gradient * negative_slope(waveform), 0.0
    ) + jnp.pad(gradient_value.astype(jnp.float32), ((DILATION_SIZE, DILATION_SIZE), (0, 0)))
    waveform_gradient = waveform_gradient.astype(jnp.bfloat16)
    d_upper = jnp.pad(waveform_gradient, ((start_offset, start_offset), (0, 0))).reshape(
        frame_count + 1, UPSAMPLE_FACTOR, window_width
    )
    zero_row = jnp.zeros((1, UPSAMPLE_FACTOR, window_width), jnp.bfloat16)
    d_taps = jnp.concatenate(
        [
            jnp.concatenate([zero_row, d_upper], axis=0),
            jnp.concatenate([d_upper, zero_row], axis=0),
        ],
        axis=1,
    )
    d_act = ups_backward(d_taps.reshape(frame_count + 2, 2 * UPSAMPLE_FACTOR * window_width))
    d_pre = jnp.where(inside_f, d_act * negative_slope(pre), 0.0).astype(jnp.bfloat16)
    g_wpre = contract_rows(patches, d_pre)
    g_bpre = jnp.sum(d_pre.astype(jnp.float32), axis=0)
    return (output_rows, (g_wpre, g_bpre, g_wres, g_bres))


def on_device(
    src_mel, owner, dst_pos, keep, cotangent, w_pre, b_pre, w_ups, upsample_bias, w_res, b_res
):
    owners_count = lax.axis_size("dp")
    seg_rows = src_mel[0]
    seg_count = seg_rows.shape[0]
    mel_bins = w_pre.shape[0] // KPRE
    pick = jnp.arange(owners_count, dtype=jnp.int32)[:, None] == owner[0][None, :]
    seg_width = seg_rows.shape[1]
    header = jnp.stack([dst_pos[0] + 1, keep[0]], axis=1).astype(jnp.bfloat16)
    seg_ext = jnp.concatenate([seg_rows, header], axis=1)
    outgoing = jnp.dot(
        pick.astype(jnp.bfloat16), seg_ext, preferred_element_type=jnp.float32
    ).astype(jnp.bfloat16)
    arrived = lax.all_to_all(outgoing, "dp", split_axis=0, concat_axis=0, tiled=True)
    slot_code = arrived[:, seg_width].astype(jnp.int32)
    keep_code = arrived[:, seg_width + 1].astype(jnp.int32)
    place = (slot_code - 1)[:, None] == jnp.arange(seg_count, dtype=jnp.int32)[None, :]
    mel_segs = contract_rows(place.astype(jnp.bfloat16), arrived[:, :seg_width]).astype(
        jnp.bfloat16
    )
    keep_segs = jnp.sum(jnp.where(place, keep_code[:, None], 0), axis=0)
    mel = mel_segs.reshape(seg_count * (mel_segs.shape[1] // mel_bins), mel_bins)
    frame_count = mel.shape[0]
    mel_ext = with_halo(mel, (("tm", 0),), KPRE // 2 + 1)
    first_frame0 = lax.axis_index("tm") * frame_count
    total = lax.axis_size("tm") * frame_count
    cot = cotangent[0]
    marks = jnp.repeat(keep_segs, cot.shape[0] // seg_count)
    gradient_value = jnp.where(marks[:, None] > 0, cot, jnp.zeros_like(cot))
    whole = lax.all_gather(w_ups, "tm", axis=0, tiled=True)

    def ups_forward(act):
        return jnp.dot(act, whole, preferred_element_type=jnp.float32)

    def ups_backward(d_taps):
        return contract_cols(d_taps, whole)

    output_rows, grads = local_pass(
        mel_ext,
        gradient_value,
        first_frame0,
        total,
        w_pre,
        b_pre,
        ups_forward,
        ups_backward,
        upsample_bias,
        w_res,
        b_res,
    )
    summed = lax.psum(grads, ("dp", "tm"))
    return (output_rows[None], summed[0], summed[1], summed[2], summed[3])


def solution(mesh):
    in_specs = (
        P("tm", "dp", None),
        P("tm", "dp"),
        P("tm", "dp"),
        P("tm", "dp"),
        P("dp", "tm", None),
        P(),
        P(),
        P("tm", None),
        P(),
        P(),
        P(),
    )
    out_specs = (P("dp", "tm", None), P(), P(), P(), P())
    return jax.shard_map(
        on_device, mesh=mesh, in_specs=in_specs, out_specs=out_specs, check_vma=False
    )
```

profile of v0, /device:TPU:0, one launch (start us, length us, event | category | flops | bytes accessed | tf_op | source)
XLA Modules:
  0.0 224.1 jit_solution(13383541488804429791)
XLA Ops:
  7.3 0.7 all-gather.2.cloned.1.call-update
  8.4 0.5 broadcast.94
  8.9 0.7 reduce.4
  9.6 0.7 reshape.74
  10.3 7.4 %all-to-all-start = ((bf16[16,2,321]{2,1,0:T(2,128)(2,1)}), bf16[16,2,321]{2,1,0:T(2,128)(2,1)S(1)}, u32[]{:S(2)}, u32[]{:S(2)}) async-start(bf16[16,2,321]{2,1,0:T(2,128)(2,1)} %reshape.74), calls=%async_computation | async-start | bytes 49152 | tf_op jit(solution)/shard_map/all_to_all | solution.py:147
  17.7 6.5 %all-to-all-done = bf16[16,2,321]{2,1,0:T(2,128)(2,1)S(1)} async-done(((bf16[16,2,321]{2,1,0:T(2,128)(2,1)}), bf16[16,2,321]{2,1,0:T(2,128)(2,1)S(1)}, u32[]{:S(2)}, u32[]{:S(2)}) %all-to-all-start) | async-done | bytes 20576 | tf_op jit(solution)/shard_map/all_to_all | solution.py:147
  24.7 1.3 collective-permute-start.1
  26.5 0.4 fusion.43
  27.1 4.5 %collective-permute-start = (bf16[4,80]{1,0:T(4,128)(2,1)S(1)}, bf16[4,80]{1,0:T(4,128)(2,1)S(1)}, u32[]{:S(2)}, u32[]{:S(2)}) collective-permute-start(bf16[4,80]{1,0:T(4,128)(2,1)S(1)} %get-tuple-element.27), channel_id=1, source_target_pairs={{0,1},{2,3},{4,5},{6,7},{8,9},{10,11},{12,13},{14,15},{16,17},{18,... | collective-permute-start | bytes 1928 | tf_op jit(solution)/shard_map/ppermute | solution.py:16
  31.6 1.3 collective-permute-done
  33.4 35.7 %all-gather.2.cloned.1.call-done = bf16[512,4096]{1,0:T(8,128)(2,1)} async-done(((bf16[256,4096]{1,0:T(8,128)(2,1)}), bf16[512,4096]{1,0:T(8,128)(2,1)}) %all-gather.2.cloned.1.call-update) | async-done | bytes 4194320 | tf_op jit(solution)/shard_map/all_gather | solution.py:163
  69.1 3.1 %fusion.19 = f32[66,4096]{1,0:T(8,128)S(1)} fusion(bf16[512,4096]{1,0:T(8,128)(2,1)} %all-gather.2.cloned.1.call-done, f32[66,512]{1,0:T(8,128)S(1)} %convolution_add_fusion.1, pred[66]{0:T(512)(128)(4,1)S(1)} %compare_and_fusion), kind=kOutput, calls=%fused_computation.37 | convolution fusion | flops 276993024 | bytes 5410882 | tf_op jit(solution)/shard_map/dot_general | solution.py:166
  72.2 0.4 copy.30
  72.8 0.5 copy-done.12
  73.3 0.3 fusion.12
  74.3 1.7 copy-done.1
  76.0 1.4 convert_reduce_fusion
  77.4 1.3 fusion.48
  78.7 1.4 fusion.16
  80.3 39.7 %all-reduce.7 = (f32[512]{0:T(512)}, f32[256]{0:T(256)}) all-reduce(f32[512]{0:T(512)S(1)} %get-tuple-element.28, f32[256]{0:T(256)S(1)} %convert_reduce_fusion.1), channel_id=1, replica_groups=mesh['dp'=16,'tm'=2] {'dp','tm'}, use_global_device_ids=true, to_apply=%region_3.4 | all-reduce | flops 768 | bytes 6144 | tf_op jit(solution)/shard_map/psum | solution.py:184
  120.0 1.1 fusion.2
  121.1 92.8 %all-reduce.11.cloned.1.call-done = (f32[560,512]{1,0:T(8,128)}, f32[768,256]{1,0:T(8,128)}) async-done(((f32[560,512]{1,0:T(8,128)}, f32[768,256]{1,0:T(8,128)}), (f32[560,512]{1,0:T(8,128)}, f32[768,256]{1,0:T(8,128)})) %all-reduce.11.cloned.1.call-update) | async-done | bytes 1933328 | tf_op jit(solution)/shard_map/psum | solution.py:184
  213.9 2.4 %copy.38 = f32[560,512]{1,0:T(8,128)} copy(f32[560,512]{1,0:T(8,128)} %get-tuple-element.31) | data formatting | bytes 2293760
  216.3 0.9 copy.39
  (70 shorter events, 3.0 us)
Async XLA Ops:
  7.2 25.9 %copy-start = (bf16[560,512]{1,0:T(8,128)(2,1)S(1)}, bf16[560,512]{1,0:T(8,128)(2,1)}, u32[]{:S(2)}) copy-start(bf16[560,512]{1,0:T(8,128)(2,1)} %param.16) | copy-start | bytes 1720324
  7.2 0.8 copy-start.15
  7.2 0.9 copy-start.16
  7.2 1.0 copy-start.13
  7.2 1.0 copy-start.10
  7.2 19.1 %copy-start.2 = (bf16[1,512,256]{2,1,0:T(8,128)(2,1)S(1)}, bf16[1,512,256]{2,1,0:T(8,128)(2,1)}, u32[]{:S(2)}) copy-start(bf16[1,512,256]{2,1,0:T(8,128)(2,1)} %param.15) | copy-start | bytes 786436
  7.2 19.3 %copy-start.8 = (bf16[768,256]{1,0:T(8,128)(2,1)S(1)}, bf16[768,256]{1,0:T(8,128)(2,1)}, u32[]{:S(2)}) copy-start(bf16[768,256]{1,0:T(8,128)(2,1)} %param.20) | copy-start | bytes 1179652
  7.2 61.9 %all-gather.2.cloned.1.call-start = ((), (), s32[]{:S(2)}) async-start(), calls=%async_computation.1 | async-start | bytes 6291456 | tf_op jit(solution)/shard_map/all_gather | solution.py:163
  10.3 13.9 %all-to-all-start = ((bf16[16,2,321]{2,1,0:T(2,128)(2,1)}), bf16[16,2,321]{2,1,0:T(2,128)(2,1)S(1)}, u32[]{:S(2)}, u32[]{:S(2)}) async-start(bf16[16,2,321]{2,1,0:T(2,128)(2,1)} %reshape.74), calls=%async_computation | async-start | bytes 49152 | tf_op jit(solution)/shard_map/all_to_all | solution.py:147
  17.6 196.3 %all-reduce.11.cloned.1.call-start = ((), (), s32[]{:S(2)}) async-start(), calls=%async_computation.2 | async-start | bytes 3866624 | tf_op jit(solution)/shard_map/psum | solution.py:184
  24.7 6.9 %collective-permute-start.1 = (bf16[4,80]{1,0:T(4,128)(2,1)S(1)}, bf16[4,80]{1,0:T(4,128)(2,1)S(1)}, u32[]{:S(2)}, u32[]{:S(2)}) collective-permute-start(bf16[4,80]{1,0:T(4,128)(2,1)S(1)} %get-tuple-element.26), channel_id=1, source_target_pairs={{1,0},{3,2},{5,4},{7,6},{9,8},{11,10},{13,12},{15,14},{17,16},{19,... | collective-permute-start | bytes 1928 | tf_op jit(solution)/shard_map/ppermute | solution.py:19
  26.9 6.2 %copy-start.11 = (f32[512]{0:T(512)S(1)}, f32[512]{0:T(512)}, u32[]{:S(2)}) copy-start(f32[512]{0:T(512)} %param.17) | copy-start | bytes 6148
  27.1 5.8 %collective-permute-start = (bf16[4,80]{1,0:T(4,128)(2,1)S(1)}, bf16[4,80]{1,0:T(4,128)(2,1)S(1)}, u32[]{:S(2)}, u32[]{:S(2)}) collective-permute-start(bf16[4,80]{1,0:T(4,128)(2,1)S(1)} %get-tuple-element.27), channel_id=1, source_target_pairs={{0,1},{2,3},{4,5},{6,7},{8,9},{10,11},{12,13},{14,15},{16,17},{18,... | collective-permute-start | bytes 1928 | tf_op jit(solution)/shard_map/ppermute | solution.py:16
  33.1 39.1 %copy-start.5 = (bf16[66,560]{1,0:T(8,128)(2,1)}, bf16[66,560]{1,0:T(8,128)(2,1)S(1)}, u32[]{:S(2)}) copy-start(bf16[66,560]{1,0:T(8,128)(2,1)S(1)} %concatenate.36) | copy-start | bytes 221764
  33.4 38.8 %copy-start.3 = (f32[66,512]{1,0:T(8,128)}, f32[66,512]{1,0:T(8,128)S(1)}, u32[]{:S(2)}) copy-start(f32[66,512]{1,0:T(8,128)S(1)} %convolution_add_fusion.1) | copy-start | bytes 405508
  72.6 0.7 copy-start.12
  73.8 2.2 copy-start.1
  74.0 2.0 copy-start.4
  76.0 1.4 copy-start.6
  80.1 39.9 %copy-start.9 = (bf16[768,256]{1,0:T(8,128)(2,1)S(1)}, bf16[768,256]{1,0:T(8,128)(2,1)}, u32[]{:S(2)}) copy-start(bf16[768,256]{1,0:T(8,128)(2,1)} %param.20) | copy-start | bytes 1179652
  80.1 39.9 %copy-start.14 = (f32[256]{0:T(256)S(1)}, f32[256]{0:T(256)}, u32[]{:S(2)}) copy-start(f32[256]{0:T(256)} %param.21) | copy-start | bytes 3076
  213.9 2.4 %copy-start.7 = (f32[768,256]{1,0:T(8,128)S(1)}, f32[768,256]{1,0:T(8,128)}, u32[]{:S(2)}) copy-start(f32[768,256]{1,0:T(8,128)} %get-tuple-element.33) | copy-start | bytes 2359300
Sparse Core Ops, SparseCore 0:
  9.6 59.4 all-gather.1
  80.3 133.6 all-reduce.10
where the time goes:
time: 224 us
  waiting for transfers between devices  137 us (61%)
  blocking collectives  39.7 us (18%)
  between operations  14.4 us (6%)
  starting transfers between devices  13.3 us (6%)
  matrix products  9.26 us (4%)
  local copies, waits for them, and re-layouts  8.51 us (4%)
    psum x1, waiting for transfers between devices, on_device(): summed = lax.psum(grads, ('dp', 'tm'))  92.8 us
    psum x1, blocking collectives, on_device(): summed = lax.psum(grads, ('dp', 'tm'))  39.7 us
    all_gather x1, waiting for transfers between devices, on_device(): whole = lax.all_gather(w_ups, 'tm', axis=0, tiled=True)  35.7 us
    all_to_all x1, starting transfers between devices, on_device(): lax.all_to_all(outgoing, 'dp', split_axis=0, concat_axis=0, tiled=True)  7.36 us
    unnamed x43, local copies, waits for them, and re-layouts  7 us
    all_to_all x1, waiting for transfers between devices, on_device(): lax.all_to_all(outgoing, 'dp', split_axis=0, concat_axis=0, tiled=True)  6.48 us
    ppermute x1, starting transfers between devices, with_halo(): lax.ppermute(lax.slice_in_dim(block, block.shape[dim] - width, None, axis...  4.54 us
  transfers between devices with their start and end apart: 5, of which 4 were waited for; matrix products, arithmetic and copies ran while one was open for 2% of the time, Pallas kernels for 0%

commit v1 on v0

--- a/solution.py
+++ b/solution.py
@@ -144,7 +144,18 @@
     outgoing = jnp.dot(
         pick.astype(jnp.bfloat16), seg_ext, preferred_element_type=jnp.float32
     ).astype(jnp.bfloat16)
-    arrived = lax.all_to_all(outgoing, "dp", split_axis=0, concat_axis=0, tiled=True)
+    ways, here = (lax.axis_size("dp"), lax.axis_index("dp"))
+    width_2 = outgoing.shape[0] // ways
+    shape = list(outgoing.shape)
+    shape[0] = width_2
+    height = shape[0]
+    shape[0] = height * ways
+    arrived = jnp.zeros(shape, outgoing.dtype)
+    for mask in range(ways):
+        part = lax.dynamic_slice_in_dim(outgoing, (here ^ mask) * width_2, width_2, axis=0)
+        if mask:
+            part = lax.ppermute(part, "dp", [(d, d ^ mask) for d in range(ways)])
+        arrived = lax.dynamic_update_slice_in_dim(arrived, part, (here ^ mask) * height, axis=0)
     slot_code = arrived[:, seg_width].astype(jnp.int32)
     keep_code = arrived[:, seg_width + 1].astype(jnp.int32)
     place = (slot_code - 1)[:, None] == jnp.arange(seg_count, dtype=jnp.int32)[None, :]

time: 224 us -> 224 us (level)
  waiting for transfers between devices: 137 us -> 102 us
  local copies, waits for them, and re-layouts: 8.51 us -> 28.9 us
  starting transfers between devices: 13.3 us -> 28.6 us
    all_gather x1, waiting for transfers between devices: 35.7 us -> 6.93 us  [on_device(): whole = lax.all_gather(w_ups, 'tm', axis=0, tiled=True)]
    ppermute x0 -> x15, starting transfers between devices: none -> 22.6 us  [on_device(): part = lax.ppermute(part, 'dp', [(d, d ^ mask) for d in range(ways)])]
    dynamic_update_slice x0 -> x16, local copies, waits for them, and re-layouts: none -> 18.7 us  [on_device(): lax.dynamic_update_slice_in_dim(arrived, part, (here ^ mask) * height, ax...]
    all_to_all x1 -> x0, starting transfers between devices: 7.36 us -> none  [on_device(): lax.all_to_all(outgoing, 'dp', split_axis=0, concat_axis=0, tiled=True)]
    all_to_all x1 -> x0, waiting for transfers between devices: 6.48 us -> none  [on_device(): lax.all_to_all(outgoing, 'dp', split_axis=0, concat_axis=0, tiled=True)]
    ppermute x0 -> x15, local copies, waits for them, and re-layouts: none -> 2.8 us  [on_device(): part = lax.ppermute(part, 'dp', [(d, d ^ mask) for d in range(ways)])]
    unnamed x43 -> x40, local copies, waits for them, and re-layouts: 7 us -> 6.14 us
  transfers between devices with their start and end apart: 5 -> 19, of which waited for: 4 -> 3; matrix products, arithmetic and copies ran while one was open for 2% -> 11% of each run, Pallas kernels for 0% -> 0%
where the time goes in v1:
time: 224 us
  waiting for transfers between devices  102 us (46%)
  blocking collectives  39.7 us (18%)
  local copies, waits for them, and re-layouts  28.9 us (13%)
  starting transfers between devices  28.6 us (13%)
  between operations  14.7 us (7%)
  matrix products  9.31 us (4%)
    psum x1, waiting for transfers between devices, on_device(): summed = lax.psum(grads, ('dp', 'tm'))  92.8 us
    psum x1, blocking collectives, on_device(): summed = lax.psum(grads, ('dp', 'tm'))  39.7 us
    ppermute x15, starting transfers between devices, on_device(): part = lax.ppermute(part, 'dp', [(d, d ^ mask) for d in range(ways)])  22.6 us
    dynamic_update_slice x16, local copies, waits for them, and re-layouts, on_device(): lax.dynamic_update_slice_in_dim(arrived, part, (here ^ mask) * height, ax...  18.7 us
    all_gather x1, waiting for transfers between devices, on_device(): whole = lax.all_gather(w_ups, 'tm', axis=0, tiled=True)  6.93 us
    unnamed x40, local copies, waits for them, and re-layouts  6.14 us
    ppermute x1, starting transfers between devices, with_halo(): lax.ppermute(lax.slice_in_dim(block, block.shape[dim] - width, None, axis...  4.56 us
  transfers between devices with their start and end apart: 19, of which 3 were waited for; matrix products, arithmetic and copies ran while one was open for 11% of the time, Pallas kernels for 0%

profile of v1, /device:TPU:0, one launch (start us, length us, event | category | flops | bytes accessed | tf_op | source)
XLA Modules:
  0.0 224.0 jit_solution(10406328389508127171)
XLA Ops:
  9.1 2.6 %collective-permute-start.1 = (bf16[1,642]{1,0:T(2,128)(2,1)S(1)}, bf16[1,642]{1,0:T(2,128)(2,1)S(1)}, u32[]{:S(2)}, u32[]{:S(2)}) collective-permute-start(bf16[1,642]{1,0:T(2,128)(2,1)S(1)} %get-tuple-element.30), channel_id=1, source_target_pairs={{0,4},{2,6},{4,0},{6,2},{8,12},{10,14},{12,8},{14,10},{16,20},{18,... | collective-permute-start | bytes 3860 | tf_op jit(solution)/shard_map/ppermute | solution.py:157
  11.7 1.8 collective-permute-start.3
  13.6 2.7 %collective-permute-start.5 = (bf16[1,642]{1,0:T(2,128)(2,1)S(1)}, bf16[1,642]{1,0:T(2,128)(2,1)S(1)}, u32[]{:S(2)}, u32[]{:S(2)}) collective-permute-start(bf16[1,642]{1,0:T(2,128)(2,1)S(1)} %get-tuple-element.26), channel_id=1, source_target_pairs={{0,12},{2,14},{4,8},{6,10},{8,4},{10,6},{12,0},{14,2},{16,28},{18,... | collective-permute-start | bytes 3860 | tf_op jit(solution)/shard_map/ppermute | solution.py:157
  16.4 2.6 %collective-permute-start.7 = (bf16[1,642]{1,0:T(2,128)(2,1)S(1)}, bf16[1,642]{1,0:T(2,128)(2,1)S(1)}, u32[]{:S(2)}, u32[]{:S(2)}) collective-permute-start(bf16[1,642]{1,0:T(2,128)(2,1)S(1)} %get-tuple-element.24), channel_id=1, source_target_pairs={{0,16},{2,18},{4,20},{6,22},{8,24},{10,26},{12,28},{14,30},{16,0},... | collective-permute-start | bytes 3860 | tf_op jit(solution)/shard_map/ppermute | solution.py:157
  19.1 3.5 %collective-permute-start.9 = (bf16[1,642]{1,0:T(2,128)(2,1)S(1)}, bf16[1,642]{1,0:T(2,128)(2,1)S(1)}, u32[]{:S(2)}, u32[]{:S(2)}) collective-permute-start(bf16[1,642]{1,0:T(2,128)(2,1)S(1)} %get-tuple-element.22), channel_id=1, source_target_pairs={{0,20},{2,22},{4,16},{6,18},{8,28},{10,30},{12,24},{14,26},{16,4},... | collective-permute-start | bytes 3860 | tf_op jit(solution)/shard_map/ppermute | solution.py:157
  23.7 1.2 dynamic_update_slice.49
  25.1 1.2 dynamic_update_slice.50
  28.2 3.6 %collective-permute-start.11 = (bf16[1,642]{1,0:T(2,128)(2,1)S(1)}, bf16[1,642]{1,0:T(2,128)(2,1)S(1)}, u32[]{:S(2)}, u32[]{:S(2)}) collective-permute-start(bf16[1,642]{1,0:T(2,128)(2,1)S(1)} %get-tuple-element.20), channel_id=1, source_target_pairs={{0,24},{2,26},{4,28},{6,30},{8,16},{10,18},{12,20},{14,22},{16,8},... | collective-permute-start | bytes 3860 | tf_op jit(solution)/shard_map/ppermute | solution.py:157
  31.9 4.4 %collective-permute-start.13 = (bf16[1,642]{1,0:T(2,128)(2,1)S(1)}, bf16[1,642]{1,0:T(2,128)(2,1)S(1)}, u32[]{:S(2)}, u32[]{:S(2)}) collective-permute-start(bf16[1,642]{1,0:T(2,128)(2,1)S(1)} %get-tuple-element.18), channel_id=1, source_target_pairs={{0,28},{2,30},{4,24},{6,26},{8,20},{10,22},{12,16},{14,18},{16,12}... | collective-permute-start | bytes 3860 | tf_op jit(solution)/shard_map/ppermute | solution.py:157
  36.6 1.2 dynamic_update_slice.52
  38.0 1.2 dynamic_update_slice.53
  49.1 1.4 dynamic_update_slice.61
  53.5 1.3 collective-permute-start.16
  55.8 4.6 %collective-permute-start.15 = (bf16[4,80]{1,0:T(4,128)(2,1)S(1)}, bf16[4,80]{1,0:T(4,128)(2,1)S(1)}, u32[]{:S(2)}, u32[]{:S(2)}) collective-permute-start(bf16[4,80]{1,0:T(4,128)(2,1)S(1)} %get-tuple-element.41), channel_id=1, source_target_pairs={{0,1},{2,3},{4,5},{6,7},{8,9},{10,11},{12,13},{14,15},{16,17},{18,... | collective-permute-start | bytes 1928 | tf_op jit(solution)/shard_map/ppermute | solution.py:16
  60.4 1.3 collective-permute-done.15
  62.2 6.9 %all-gather.2.cloned.1.call-done = bf16[512,4096]{1,0:T(8,128)(2,1)} async-done(((bf16[256,4096]{1,0:T(8,128)(2,1)}), bf16[512,4096]{1,0:T(8,128)(2,1)}) %all-gather.2.cloned.1.call-update) | async-done | bytes 4194320 | tf_op jit(solution)/shard_map/all_gather | solution.py:174
  69.1 3.1 %fusion.19 = f32[66,4096]{1,0:T(8,128)S(1)} fusion(bf16[512,4096]{1,0:T(8,128)(2,1)} %all-gather.2.cloned.1.call-done, f32[66,512]{1,0:T(8,128)S(1)} %convolution_add_fusion.1, pred[66]{0:T(512)(128)(4,1)S(1)} %compare_and_fusion), kind=kOutput, calls=%fused_computation.37 | convolution fusion | flops 276993024 | bytes 5410882 | tf_op jit(solution)/shard_map/dot_general | solution.py:177
  74.3 1.6 copy-done.1
  75.9 1.4 convert_reduce_fusion
  77.3 1.3 fusion.50
  78.7 1.4 fusion.15
  80.2 39.7 %all-reduce.7 = (f32[512]{0:T(512)}, f32[256]{0:T(256)}) all-reduce(f32[512]{0:T(512)S(1)} %get-tuple-element.42, f32[256]{0:T(256)S(1)} %convert_reduce_fusion.1), channel_id=1, replica_groups=mesh['dp'=16,'tm'=2] {'dp','tm'}, use_global_device_ids=true, to_apply=%region_3.4 | all-reduce | flops 768 | bytes 6144 | tf_op jit(solution)/shard_map/psum | solution.py:195
  121.0 92.8 %all-reduce.11.cloned.1.call-done = (f32[560,512]{1,0:T(8,128)}, f32[768,256]{1,0:T(8,128)}) async-done(((f32[560,512]{1,0:T(8,128)}, f32[768,256]{1,0:T(8,128)}), (f32[560,512]{1,0:T(8,128)}, f32[768,256]{1,0:T(8,128)})) %all-reduce.11.cloned.1.call-update) | async-done | bytes 1933328 | tf_op jit(solution)/shard_map/psum | solution.py:195
  213.9 2.4 %copy.73 = f32[560,512]{1,0:T(8,128)} copy(f32[560,512]{1,0:T(8,128)} %get-tuple-element.45) | data formatting | bytes 2293760
  (128 shorter events, 24.2 us)
Async XLA Ops:
  7.2 54.7 %copy-start = (bf16[560,512]{1,0:T(8,128)(2,1)S(1)}, bf16[560,512]{1,0:T(8,128)(2,1)}, u32[]{:S(2)}) copy-start(bf16[560,512]{1,0:T(8,128)(2,1)} %param.16) | copy-start | bytes 1720324
  7.2 61.9 %all-gather.2.cloned.1.call-start = ((), (), s32[]{:S(2)}) async-start(), calls=%async_computation | async-start | bytes 6291456 | tf_op jit(solution)/shard_map/all_gather | solution.py:174
  8.0 205.9 %all-reduce.11.cloned.1.call-start = ((), (), s32[]{:S(2)}) async-start(), calls=%async_computation.1 | async-start | bytes 3866624 | tf_op jit(solution)/shard_map/psum | solution.py:195
  8.6 5.0 %collective-permute-start = (bf16[1,642]{1,0:T(2,128)(2,1)S(1)}, bf16[1,642]{1,0:T(2,128)(2,1)S(1)}, u32[]{:S(2)}, u32[]{:S(2)}) collective-permute-start(bf16[1,642]{1,0:T(2,128)(2,1)S(1)} %get-tuple-element.31), channel_id=1, source_target_pairs={{0,2},{2,0},{4,6},{6,4},{8,10},{10,8},{12,14},{14,12},{16,18},{18,... | collective-permute-start | bytes 3860 | tf_op jit(solution)/shard_map/ppermute | solution.py:157
  9.1 7.2 %collective-permute-start.1 = (bf16[1,642]{1,0:T(2,128)(2,1)S(1)}, bf16[1,642]{1,0:T(2,128)(2,1)S(1)}, u32[]{:S(2)}, u32[]{:S(2)}) collective-permute-start(bf16[1,642]{1,0:T(2,128)(2,1)S(1)} %get-tuple-element.30), channel_id=1, source_target_pairs={{0,4},{2,6},{4,0},{6,2},{8,12},{10,14},{12,8},{14,10},{16,20},{18,... | collective-permute-start | bytes 3860 | tf_op jit(solution)/shard_map/ppermute | solution.py:157
  11.7 4.7 %collective-permute-start.2 = (bf16[1,642]{1,0:T(2,128)(2,1)S(1)}, bf16[1,642]{1,0:T(2,128)(2,1)S(1)}, u32[]{:S(2)}, u32[]{:S(2)}) collective-permute-start(bf16[1,642]{1,0:T(2,128)(2,1)S(1)} %get-tuple-element.29), channel_id=1, source_target_pairs={{0,6},{2,4},{4,2},{6,0},{8,14},{10,12},{12,10},{14,8},{16,22},{18,... | collective-permute-start | bytes 3860 | tf_op jit(solution)/shard_map/ppermute | solution.py:157
  11.7 7.3 %collective-permute-start.3 = (bf16[1,642]{1,0:T(2,128)(2,1)S(1)}, bf16[1,642]{1,0:T(2,128)(2,1)S(1)}, u32[]{:S(2)}, u32[]{:S(2)}) collective-permute-start(bf16[1,642]{1,0:T(2,128)(2,1)S(1)} %get-tuple-element.28), channel_id=1, source_target_pairs={{0,8},{2,10},{4,12},{6,14},{8,0},{10,2},{12,4},{14,6},{16,24},{18,... | collective-permute-start | bytes 3860 | tf_op jit(solution)/shard_map/ppermute | solution.py:157
  13.6 5.5 %collective-permute-start.4 = (bf16[1,642]{1,0:T(2,128)(2,1)S(1)}, bf16[1,642]{1,0:T(2,128)(2,1)S(1)}, u32[]{:S(2)}, u32[]{:S(2)}) collective-permute-start(bf16[1,642]{1,0:T(2,128)(2,1)S(1)} %get-tuple-element.27), channel_id=1, source_target_pairs={{0,10},{2,8},{4,14},{6,12},{8,2},{10,0},{12,6},{14,4},{16,26},{18,... | collective-permute-start | bytes 3860 | tf_op jit(solution)/shard_map/ppermute | solution.py:157
  13.6 14.1 %collective-permute-start.5 = (bf16[1,642]{1,0:T(2,128)(2,1)S(1)}, bf16[1,642]{1,0:T(2,128)(2,1)S(1)}, u32[]{:S(2)}, u32[]{:S(2)}) collective-permute-start(bf16[1,642]{1,0:T(2,128)(2,1)S(1)} %get-tuple-element.26), channel_id=1, source_target_pairs={{0,12},{2,14},{4,8},{6,10},{8,4},{10,6},{12,0},{14,2},{16,28},{18,... | collective-permute-start | bytes 3860 | tf_op jit(solution)/shard_map/ppermute | solution.py:157
  16.2 12.0 %collective-permute-start.6 = (bf16[1,642]{1,0:T(2,128)(2,1)S(1)}, bf16[1,642]{1,0:T(2,128)(2,1)S(1)}, u32[]{:S(2)}, u32[]{:S(2)}) collective-permute-start(bf16[1,642]{1,0:T(2,128)(2,1)S(1)} %get-tuple-element.25), channel_id=1, source_target_pairs={{0,14},{2,12},{4,10},{6,8},{8,6},{10,4},{12,2},{14,0},{16,30},{18,... | collective-permute-start | bytes 3860 | tf_op jit(solution)/shard_map/ppermute | solution.py:157
  16.4 15.5 %collective-permute-start.7 = (bf16[1,642]{1,0:T(2,128)(2,1)S(1)}, bf16[1,642]{1,0:T(2,128)(2,1)S(1)}, u32[]{:S(2)}, u32[]{:S(2)}) collective-permute-start(bf16[1,642]{1,0:T(2,128)(2,1)S(1)} %get-tuple-element.24), channel_id=1, source_target_pairs={{0,16},{2,18},{4,20},{6,22},{8,24},{10,26},{12,28},{14,30},{16,0},... | collective-permute-start | bytes 3860 | tf_op jit(solution)/shard_map/ppermute | solution.py:157
  19.0 12.9 %collective-permute-start.8 = (bf16[1,642]{1,0:T(2,128)(2,1)S(1)}, bf16[1,642]{1,0:T(2,128)(2,1)S(1)}, u32[]{:S(2)}, u32[]{:S(2)}) collective-permute-start(bf16[1,642]{1,0:T(2,128)(2,1)S(1)} %get-tuple-element.23), channel_id=1, source_target_pairs={{0,18},{2,16},{4,22},{6,20},{8,26},{10,24},{12,30},{14,28},{16,2},... | collective-permute-start | bytes 3860 | tf_op jit(solution)/shard_map/ppermute | solution.py:157
  19.1 17.2 %collective-permute-start.9 = (bf16[1,642]{1,0:T(2,128)(2,1)S(1)}, bf16[1,642]{1,0:T(2,128)(2,1)S(1)}, u32[]{:S(2)}, u32[]{:S(2)}) collective-permute-start(bf16[1,642]{1,0:T(2,128)(2,1)S(1)} %get-tuple-element.22), channel_id=1, source_target_pairs={{0,20},{2,22},{4,16},{6,18},{8,28},{10,30},{12,24},{14,26},{16,4},... | collective-permute-start | bytes 3860 | tf_op jit(solution)/shard_map/ppermute | solution.py:157
  27.7 18.4 %collective-permute-start.10 = (bf16[1,642]{1,0:T(2,128)(2,1)S(1)}, bf16[1,642]{1,0:T(2,128)(2,1)S(1)}, u32[]{:S(2)}, u32[]{:S(2)}) collective-permute-start(bf16[1,642]{1,0:T(2,128)(2,1)S(1)} %get-tuple-element.21), channel_id=1, source_target_pairs={{0,22},{2,20},{4,18},{6,16},{8,30},{10,28},{12,26},{14,24},{16,6},... | collective-permute-start | bytes 3860 | tf_op jit(solution)/shard_map/ppermute | solution.py:157
  28.2 19.2 %collective-permute-start.11 = (bf16[1,642]{1,0:T(2,128)(2,1)S(1)}, bf16[1,642]{1,0:T(2,128)(2,1)S(1)}, u32[]{:S(2)}, u32[]{:S(2)}) collective-permute-start(bf16[1,642]{1,0:T(2,128)(2,1)S(1)} %get-tuple-element.20), channel_id=1, source_target_pairs={{0,24},{2,26},{4,28},{6,30},{8,16},{10,18},{12,20},{14,22},{16,8},... | collective-permute-start | bytes 3860 | tf_op jit(solution)/shard_map/ppermute | solution.py:157
  31.9 17.0 %collective-permute-start.12 = (bf16[1,642]{1,0:T(2,128)(2,1)S(1)}, bf16[1,642]{1,0:T(2,128)(2,1)S(1)}, u32[]{:S(2)}, u32[]{:S(2)}) collective-permute-start(bf16[1,642]{1,0:T(2,128)(2,1)S(1)} %get-tuple-element.19), channel_id=1, source_target_pairs={{0,26},{2,24},{4,30},{6,28},{8,18},{10,16},{12,22},{14,20},{16,10}... | collective-permute-start | bytes 3860 | tf_op jit(solution)/shard_map/ppermute | solution.py:157
  31.9 18.5 %collective-permute-start.13 = (bf16[1,642]{1,0:T(2,128)(2,1)S(1)}, bf16[1,642]{1,0:T(2,128)(2,1)S(1)}, u32[]{:S(2)}, u32[]{:S(2)}) collective-permute-start(bf16[1,642]{1,0:T(2,128)(2,1)S(1)} %get-tuple-element.18), channel_id=1, source_target_pairs={{0,28},{2,30},{4,24},{6,26},{8,20},{10,22},{12,16},{14,18},{16,12}... | collective-permute-start | bytes 3860 | tf_op jit(solution)/shard_map/ppermute | solution.py:157
  36.3 15.5 %collective-permute-start.14 = (bf16[1,642]{1,0:T(2,128)(2,1)S(1)}, bf16[1,642]{1,0:T(2,128)(2,1)S(1)}, u32[]{:S(2)}, u32[]{:S(2)}) collective-permute-start(bf16[1,642]{1,0:T(2,128)(2,1)S(1)} %get-tuple-element.17), channel_id=1, source_target_pairs={{0,30},{2,28},{4,26},{6,24},{8,22},{10,20},{12,18},{14,16},{16,14}... | collective-permute-start | bytes 3860 | tf_op jit(solution)/shard_map/ppermute | solution.py:157
  44.7 10.4 %copy-start.2 = (bf16[1,512,256]{2,1,0:T(8,128)(2,1)S(1)}, bf16[1,512,256]{2,1,0:T(8,128)(2,1)}, u32[]{:S(2)}) copy-start(bf16[1,512,256]{2,1,0:T(8,128)(2,1)} %param.15) | copy-start | bytes 786436
  53.5 6.9 %collective-permute-start.16 = (bf16[4,80]{1,0:T(4,128)(2,1)S(1)}, bf16[4,80]{1,0:T(4,128)(2,1)S(1)}, u32[]{:S(2)}, u32[]{:S(2)}) collective-permute-start(bf16[4,80]{1,0:T(4,128)(2,1)S(1)} %get-tuple-element.40), channel_id=1, source_target_pairs={{1,0},{3,2},{5,4},{7,6},{9,8},{11,10},{13,12},{15,14},{17,16},{19,... | collective-permute-start | bytes 1928 | tf_op jit(solution)/shard_map/ppermute | solution.py:19
  55.8 5.8 %collective-permute-start.15 = (bf16[4,80]{1,0:T(4,128)(2,1)S(1)}, bf16[4,80]{1,0:T(4,128)(2,1)S(1)}, u32[]{:S(2)}, u32[]{:S(2)}) collective-permute-start(bf16[4,80]{1,0:T(4,128)(2,1)S(1)} %get-tuple-element.41), channel_id=1, source_target_pairs={{0,1},{2,3},{4,5},{6,7},{8,9},{10,11},{12,13},{14,15},{16,17},{18,... | collective-permute-start | bytes 1928 | tf_op jit(solution)/shard_map/ppermute | solution.py:16
  61.9 10.3 %copy-start.5 = (bf16[66,560]{1,0:T(8,128)(2,1)}, bf16[66,560]{1,0:T(8,128)(2,1)S(1)}, u32[]{:S(2)}) copy-start(bf16[66,560]{1,0:T(8,128)(2,1)S(1)} %concatenate.36) | copy-start | bytes 221764
  80.1 39.9 %copy-start.9 = (bf16[768,256]{1,0:T(8,128)(2,1)S(1)}, bf16[768,256]{1,0:T(8,128)(2,1)}, u32[]{:S(2)}) copy-start(bf16[768,256]{1,0:T(8,128)(2,1)} %param.20) | copy-start | bytes 1179652
  80.1 39.9 %copy-start.14 = (f32[256]{0:T(256)S(1)}, f32[256]{0:T(256)}, u32[]{:S(2)}) copy-start(f32[256]{0:T(256)} %param.21) | copy-start | bytes 3076
  (12 other events, 36.9 us)
Sparse Core Ops, SparseCore 0:
  9.6 59.4 all-gather.1
  80.2 133.6 all-reduce.10
